TPU v7x, 32 devices: a whole 2x2x4 slice. The times are simulated.
32 devices in a mesh: groups: 2 (over y), ctx: 4 (over z), mp: 2 (over x), sub: 2 (over core).
Axes of the slice: x: 2, y: 2, z: 4, core: 2. Of those that a mesh axis runs over, the one named last changes fastest.
Arguments:
- features: bfloat16 [16384, 3, 4096], P(('groups', 'ctx'), None, ('mp', 'sub')), parts along dimension 0, may hold values from -6 to 6
- short_filter: float32 [7, 3, 4096], P(None, None, ('mp', 'sub')), may hold values from -2 to 2
- mr_filter: bfloat16 [256, 128], P(('mp', 'sub')), may hold values from -0.5 to 0.5
- lr_gates: bfloat16 [16384, 2, 4096], P(('groups', 'ctx'), None, ('mp', 'sub')), parts along dimension 0, may hold values from -6 to 6
- lr_rate: float32 [4096, 16], P(('mp', 'sub')), may hold values from 6.1035156e-05 to 0.05
- lr_residue: float32 [4096, 16], P(('mp', 'sub')), may hold values from -2 to 2
- lr_skip: float32 [4096], P(('mp', 'sub')), may hold values from -3 to 3
Outputs:
- output: bfloat16 [16384, 4096], P(('groups', 'ctx'), ('mp', 'sub')), parts along dimension 0
There are 2 independent parts, one for each index of `groups`. A program takes and returns all parts, laid end to end along the dimension named above; an argument that names none is the same for every part. Nothing has to cross between parts.
All inputs are finite; a program needn't handle non-finite values.
Results may differ from a plain program's by a relative error of at most 0.0059.
Values may be sent and summed in bfloat16 or wider, within the bound.
No kernel may reach another device: no remote copies, remote signals or barrier semaphores. Data moves between devices by JAX's collectives and lax.ppermute only.
A program may use at most 192 MiB of HBM per device.

v0:
```python
import jax
import jax.numpy as jnp
from jax import lax
from jax.sharding import PartitionSpec as P

TAPS = 128
SHORT = 7


def passed_along(shard, axis, by):
    devices = lax.axis_size(axis)
    pairs = [(i, i + by) for i in range(devices) if 0 <= i + by < devices]
    return lax.ppermute(shard, axis, pairs)


def featurize(extended, weights):
    width = weights.shape[0]
    count = extended.shape[0] - (width - 1)
    total = jnp.zeros((count,) + extended.shape[1:], jnp.float32)
    for j in range(width):
        total = total + weights[j] * extended[width - 1 - j : width - 1 - j + count]
    return total


def medium_mix(extended, filters):
    groups, taps = filters.shape
    rows = extended.shape[0] - (taps - 1)
    chans = extended.shape[1]
    padded = jnp.concatenate([jnp.zeros((1, chans), jnp.bfloat16), extended], 0)
    blocks = rows // taps
    before = padded[:rows].reshape(blocks, taps, chans)
    current = padded[taps:].reshape(blocks, taps, chans)
    window = jnp.concatenate([before, current], 1).reshape(
        blocks, 2 * taps, groups, chans // groups
    )
    window = window.transpose(2, 3, 0, 1)
    lag = jnp.arange(taps)[:, None] + taps - jnp.arange(2 * taps)[None, :]
    valid = (lag >= 0) & (lag < taps)
    toeplitz = jnp.where(
        valid[None], filters[:, jnp.clip(lag, 0, taps - 1)], jnp.zeros((), jnp.bfloat16)
    )
    mixed = jnp.einsum("gts,gkbs->gkbt", toeplitz, window, preferred_element_type=jnp.float32)
    return mixed.transpose(2, 3, 0, 1).reshape(rows, chans)


def modal_local(signal, rate_modes, residue_modes):
    rows_block = 64
    count, chans = signal.shape
    blocks = count // rows_block
    weight = residue_modes * jnp.sqrt(rate_modes)
    steps = jnp.arange(rows_block).astype(jnp.float32)
    decay_in = jnp.exp(-rate_modes[None] * steps[:, None, None])
    kernel = jnp.einsum("trc,rc->tc", decay_in, weight, precision=lax.Precision.HIGHEST)
    lag = jnp.arange(rows_block)[:, None] - jnp.arange(rows_block)[None, :]
    toeplitz = jnp.where((lag >= 0)[:, :, None], kernel[jnp.maximum(lag, 0)], 0.0)
    blocked = signal.astype(jnp.float32).reshape(blocks, rows_block, chans)
    intra = jnp.einsum("tsc,bsc->btc", toeplitz, blocked, precision=lax.Precision.HIGHEST)
    decay_out = jnp.exp(-rate_modes[None] * (rows_block - 1 - steps)[:, None, None])
    contrib = jnp.einsum("bsc,src->brc", blocked, decay_out, precision=lax.Precision.HIGHEST)
    gap = (jnp.arange(blocks)[:, None] - jnp.arange(blocks)[None, :] - 1).astype(jnp.float32)
    before_mask = gap >= 0.0
    gap_rows = jnp.maximum(gap, 0.0) * rows_block

    def mode_prefix(pair):
        rate_one, contrib_one = pair
        decay = jnp.where(
            before_mask[:, :, None], jnp.exp(-rate_one[None, None, :] * gap_rows[:, :, None]), 0.0
        )
        return jnp.einsum("xbc,bc->xc", decay, contrib_one, precision=lax.Precision.HIGHEST)

    incoming = lax.map(mode_prefix, (rate_modes, contrib.transpose(1, 0, 2))).transpose(1, 0, 2)
    last_state = incoming[-1] * jnp.exp(-rate_modes * rows_block) + contrib[-1]
    readout = jnp.exp(-rate_modes[None] * (steps + 1.0)[:, None, None]) * weight[None]
    return (intra, incoming, last_state, readout)


def modal_finish(intra, incoming, readout):
    state = jnp.einsum("brc,trc->btc", incoming, readout, precision=lax.Precision.HIGHEST)
    return (intra + state).reshape(-1, intra.shape[2])


def per_device(features, short_filter, mr_filter, lr_gates, lr_rate, lr_residue, lr_skip):
    count = features.shape[0]
    rim = passed_along(features[count - (SHORT - 1) :], "ctx", 1)
    featured = featurize(jnp.concatenate([rim, features], 0), short_filter)
    query = featured[:, 0]
    product = (featured[:, 1] * featured[:, 2]).astype(jnp.bfloat16)
    prior = passed_along(product[count - (TAPS - 1) :], "ctx", 1)
    extended = jnp.concatenate([prior, product], 0)
    mixed = medium_mix(extended, mr_filter)
    lr_input = (lr_gates[:, 1] * query * mixed).astype(jnp.bfloat16)
    spread = lax.all_to_all(lr_input, "ctx", split_axis=1, concat_axis=0, tiled=True)
    width = spread.shape[1]
    offset = lax.axis_index("ctx") * width
    rate_modes = lax.dynamic_slice_in_dim(lr_rate, offset, width, 0).T
    residue_modes = lax.dynamic_slice_in_dim(lr_residue, offset, width, 0).T
    intra, incoming, last_state, readout = modal_local(spread, rate_modes, residue_modes)
    part_mix = modal_finish(intra, incoming, readout)
    long_mix = lax.all_to_all(part_mix, "ctx", split_axis=0, concat_axis=1, tiled=True)
    return (lr_gates[:, 0] * (long_mix + lr_skip * lr_input.astype(jnp.float32))).astype(
        jnp.bfloat16
    )


def solution(mesh):
    in_specs = (
        P(("groups", "ctx"), None, ("mp", "sub")),
        P(None, None, ("mp", "sub")),
        P(("mp", "sub"), None),
        P(("groups", "ctx"), None, ("mp", "sub")),
        P(("mp", "sub"), None),
        P(("mp", "sub"), None),
        P(("mp", "sub")),
    )
    out_specs = P(("groups", "ctx"), ("mp", "sub"))
    return jax.shard_map(
        per_device, mesh=mesh, in_specs=in_specs, out_specs=out_specs, check_vma=False
    )
```

profile of v0, /device:TPU:0, one launch (start us, length us, event | category | flops | bytes accessed | tf_op | source)
XLA Modules:
  0.0 906.1 jit_solution(622854457128697138)
XLA Ops:
  0.8 5.0 collective-permute-start
  7.3 17.8 %fusion.47 = (bf16[2048,1,1024]{2,1,0:T(2,128)(2,1)}, bf16[2048,1,1024]{2,1,0:T(2,128)(2,1)}) fusion(bf16[2048,2,1024]{2,1,0:T(2,128)(2,1)} %param.12), kind=kLoop, calls=%fused_computation.89 | loop fusion | bytes 16777216 | tf_op jit(solution)/shard_map/slice | solution.py:100
  25.2 16.9 %copy.54 = bf16[2048,3,1024]{0,2,1:T(8,128)(2,1)} copy(bf16[2048,3,1024]{2,0,1:T(8,128)(2,1)} %param.9) | data formatting | bytes 25165824 | tf_op args[0]
  42.1 19.8 %copy.94 = bf16[2048,1,1024]{0,2,1:T(8,128)(2,1)} copy(bf16[2048,1,1024]{2,1,0:T(2,128)(2,1)} %get-tuple-element.70) | data formatting | bytes 8388608
  62.5 66.6 %multiply_add_fusion = f32[2048,3,1024]{0,2,1:T(8,128)} fusion(bf16[2048,3,1024]{0,2,1:T(8,128)(2,1)} %copy.54, bf16[6,3,1024]{0,2,1:T(8,128)(2,1)S(1)} %copy.55, f32[3,1024]{1,0:T(4,128)S(1)} %get-tuple-element.78, f32[3,1024]{1,0:T(4,128)S(1)} %get-tuple-element.79, f32[3,1024]{1,0:T(4,128)S(1)} %get-tuple-element.80, f32[3,1024]{1,0:T(4,128)S(1)} %get-tuple-element.81, ...), kind=kLoop, calls=%fused_computation.15 | loop fusion | flops 239075328 | bytes 37871616 | tf_op jit(solution)/shard_map/add | solution.py:21
  129.1 14.6 %fusion.10 = (bf16[2048,1,1024]{0,2,1:T(8,128)(2,1)S(1)}, f32[2048,1,1024]{0,2,1:T(8,128)}) fusion(f32[2048,3,1024]{0,2,1:T(8,128)} %multiply_add_fusion, bf16[2048,1,1024]{0,2,1:T(8,128)(2,1)} %copy.94), kind=kLoop, calls=%fused_computation.28 | loop fusion | flops 8388608 | bytes 41943040 | tf_op jit(solution)/shard_map/convert_element_type | solution.py:87
  147.7 114.9 %gather_fusion = bf16[32768,64]{1,0:T(8,128)(2,1)} fusion(bf16[64,128]{0,1:T(8,128)(2,1)S(1)} %copy.57, s32[32768]{0:T(1024)S(1)} %broadcast_clamp_fusion), kind=kCustom, calls=%fused_computation | custom fusion | bytes 8519680 | tf_op jit(solution)/shard_map/gather | solution.py:40
  262.6 10.1 %copy.58 = bf16[128,256,64]{1,0,2:T(8,128)(2,1)} copy(bf16[128,256,64]{2,1,0:T(8,128)(2,1)} %bitcast.122) | data formatting | bytes 8388608 | tf_op jit(solution)/shard_map/gather | solution.py:40
  272.8 5.6 copy.99
  278.5 7.9 concatenate.13
  292.5 7.8 fusion.11
  300.3 9.3 %reshape.164 = f32[2048,4,256]{0,2,1:T(8,128)} reshape(f32[16,128,64,16]{1,0,3,2:T(8,128)} %bitcast.119) | data formatting | bytes 16777216 | tf_op jit(solution)/shard_map/reshape | solution.py:43
  309.6 9.2 %multiply_convert_fusion = bf16[2048,4,256]{0,2,1:T(8,128)(2,1)} fusion(f32[2048,4,256]{0,2,1:T(8,128)} %bitcast.116, f32[2048,4,256]{0,2,1:T(8,128)} %reshape.164), kind=kLoop, calls=%fused_computation.40 | loop fusion | flops 4194304 | bytes 20971520 | tf_op jit(solution)/shard_map/convert_element_type | solution.py:91
  318.8 5.1 all-to-all-start
  326.8 16.1 %gather_fusion.1 = f32[4096,256]{1,0:T(8,128)} fusion(f32[64,256]{1,0:T(8,128)S(1)} %bitcast.115, s32[4096]{0:T(1024)S(1)} %broadcast_clamp_fusion.1), kind=kCustom, calls=%fused_computation.1 | custom fusion | bytes 8404992 | tf_op jit(solution)/shard_map/gather | solution.py:55
  342.9 9.2 %copy.61 = f32[64,64,256]{1,0,2:T(8,128)} copy(f32[64,64,256]{2,1,0:T(8,128)} %bitcast.124) | data formatting | bytes 8388608 | tf_op jit(solution)/shard_map/gather | solution.py:55
  352.1 64.5 %all-to-all-done = bf16[2048,4,256]{0,2,1:T(8,128)(2,1)} async-done(((bf16[2048,4,256]{0,2,1:T(8,128)(2,1)}), bf16[2048,4,256]{0,2,1:T(8,128)(2,1)}, u32[]{:S(2)}, u32[]{:S(2)}) %all-to-all-start) | async-done | bytes 4194336 | tf_op jit(solution)/shard_map/all_to_all | solution.py:92
  416.6 6.2 copy.59
  422.8 7.4 copy.62
  430.1 5.2 fusion.32
  435.4 215.4 %while.11 = (s32[]{:T(128)}, f32[16,128,256]{1,0,2:T(8,128)}, f32[16,128,256]{1,0,2:T(8,128)S(1)}, f32[16,256]{1,0:T(8,128)S(1)}, s32[]{:T(128)}, /*index=5*/s32[]{:T(128)}) while((s32[]{:T(128)}, f32[16,128,256]{1,0,2:T(8,128)}, f32[16,128,256]{1,0,2:T(8,128)S(1)}, f32[16,256]{1,0:T(8,128)S(1)}, s32[]{:T(128)}, ...), condition=%wide.region_1.2_spmd.clone, body=%wide.region_0.1_spmd.clone.sunk | while | flops 16892160 | bytes 1477713 | solution.py:71
  435.7 8.4 multiply_reduce_fusion.3
  444.2 4.7 dynamic_update_slice.6
  449.2 8.4 multiply_reduce_fusion.3
  457.7 4.7 dynamic_update_slice.6
  462.6 8.4 multiply_reduce_fusion.3
  476.1 8.4 multiply_reduce_fusion.3
  489.5 8.4 multiply_reduce_fusion.3
  503.0 8.4 multiply_reduce_fusion.3
  516.5 8.4 multiply_reduce_fusion.3
  529.9 8.4 multiply_reduce_fusion.3
  543.4 8.4 multiply_reduce_fusion.3
  556.8 8.4 multiply_reduce_fusion.3
  570.3 8.4 multiply_reduce_fusion.3
  583.8 8.4 multiply_reduce_fusion.3
  597.2 8.4 multiply_reduce_fusion.3
  610.7 8.4 multiply_reduce_fusion.3
  624.2 8.4 multiply_reduce_fusion.3
  637.6 8.4 multiply_reduce_fusion.3
  650.8 17.9 %fusion.28 = f32[256,64,128]{2,1,0:T(8,128)} fusion(f32[16,128,256]{1,0,2:T(8,128)} %get-tuple-element.37, f32[16,256]{0,1:T(8,128)S(1)} %copy.63, f32[64]{0:T(128)S(1)} %broadcast_add_fusion, f32[16,256]{0,1:T(8,128)S(1)} %copy.60), kind=kOutput, calls=%fused_computation.52 | convolution fusion | flops 403177472 | bytes 10518784 | tf_op jit(solution)/shard_map/brc,trc->btc/dot_general | solution.py:78
  668.7 10.5 %bitcast_add_fusion.1 = f32[128,64,256]{0,1,2:T(8,128)} fusion(f32[256,64,128]{2,1,0:T(8,128)} %fusion.28, bf16[128,64,256]{0,1,2:T(8,128)(2,1)S(1)} %copy-done.1, f32[64,64,256]{1,0,2:T(8,128)} %copy.61, pred[64,64]{1,0:T(8,128)(4,1)S(1)} %subtract_compare_fusion), kind=kOutput, calls=%fused_computation.37 | convolution fusion | flops 1613758464 | bytes 25169920 | tf_op jit(solution)/shard_map/tsc,bsc->btc/dot_general | solution.py:57
  679.2 9.2 %copy.67 = f32[128,64,256]{2,1,0:T(8,128)} copy(f32[128,64,256]{0,1,2:T(8,128)} %bitcast_add_fusion.1) | data formatting | bytes 16777216 | tf_op jit(solution)/shard_map/add | solution.py:79
  688.4 5.9 all-to-all-start.1
  694.4 19.9 %copy.95 = bf16[2048,1,1024]{0,2,1:T(8,128)(2,1)} copy(bf16[2048,1,1024]{2,1,0:T(2,128)(2,1)} %get-tuple-element.69) | data formatting | bytes 8388608
  714.2 162.5 %all-to-all-done.1 = f32[4,2048,256]{2,1,0:T(8,128)} async-done(((f32[4,2048,256]{2,1,0:T(8,128)}), f32[4,2048,256]{2,1,0:T(8,128)}, u32[]{:S(2)}, u32[]{:S(2)}) %all-to-all-start.1) | async-done | bytes 8388640 | tf_op jit(solution)/shard_map/all_to_all | solution.py:99
  876.7 8.7 copy.68
  885.4 14.3 %fusion.14 = bf16[2048,1024]{0,1:T(8,128)(2,1)} fusion(f32[2048,4,256]{0,2,1:T(8,128)} %copy.68, f32[128,8,16,128]{3,2,1,0:T(8,128)} %bitcast.120, f32[2048,1,1024]{0,2,1:T(8,128)} %get-tuple-element.68, bf16[2048,1,1024]{0,2,1:T(8,128)(2,1)} %copy.95, f32[1024]{0:T(1024)S(1)} %copy-done.5), kind=kLoop, calls=%fused_computation.35 | loop fusion | flops 16777216 | bytes 33558528 | tf_op jit(solution)/shard_map/convert_element_type | solution.py:100
  899.7 6.4 copy.69
  (157 shorter events, 86.9 us)
Async XLA Ops:
  0.8 61.3 %collective-permute-start = (bf16[6,3,1024]{2,0,1:T(8,128)(2,1)S(1)}, bf16[6,3,1024]{2,0,1:T(8,128)(2,1)S(1)}, u32[]{:S(2)}, u32[]{:S(2)}) collective-permute-start(bf16[6,3,1024]{2,0,1:T(8,128)(2,1)S(1)} %slice.70), channel_id=1, source_target_pairs={{0,4},{4,8},{8,12},{1,5},{5,9},{9,13},{2,6},{6,10},{10,14},{3,7},{... | collective-permute-start | bytes 110600 | tf_op jit(solution)/shard_map/ppermute | solution.py:13
  129.1 18.5 %copy-start.4 = (bf16[64,128]{1,0:T(8,128)(2,1)S(1)}, bf16[64,128]{1,0:T(8,128)(2,1)}, u32[]{:S(2)}) copy-start(bf16[64,128]{1,0:T(8,128)(2,1)} %param.11) | copy-start | bytes 49156
  143.7 3.8 copy-start
  143.9 134.6 %collective-permute-start.1 = (bf16[127,1024]{0,1:T(8,128)(2,1)S(1)}, bf16[127,1024]{0,1:T(8,128)(2,1)S(1)}, u32[]{:S(2)}, u32[]{:S(2)}) collective-permute-start(bf16[127,1024]{0,1:T(8,128)(2,1)S(1)} %slice_bitcast_fusion.1), channel_id=1, source_target_pairs={{0,4},{4,8},{8,12},{1,5},{5,9},{9,13},{2,6},{6,10},{10,14},{3,7},{... | collective-permute-start | bytes 780296 | tf_op jit(solution)/shard_map/ppermute | solution.py:13
  286.5 6.1 copy-start.2
  286.5 6.1 copy-start.3
  318.8 97.8 %all-to-all-start = ((bf16[2048,4,256]{0,2,1:T(8,128)(2,1)}), bf16[2048,4,256]{0,2,1:T(8,128)(2,1)}, u32[]{:S(2)}, u32[]{:S(2)}) async-start(bf16[2048,4,256]{0,2,1:T(8,128)(2,1)} %multiply_convert_fusion), calls=%async_computation | async-start | bytes 8388608 | tf_op jit(solution)/shard_map/all_to_all | solution.py:92
  650.8 17.9 %copy-start.1 = (bf16[128,64,256]{0,1,2:T(8,128)(2,1)S(1)}, bf16[128,64,256]{0,1,2:T(8,128)(2,1)}, u32[]{:S(2)}) copy-start(bf16[128,64,256]{0,1,2:T(8,128)(2,1)} %copy.62) | copy-start | bytes 12582916
  688.4 188.3 %all-to-all-start.1 = ((f32[4,2048,256]{2,1,0:T(8,128)}), f32[4,2048,256]{2,1,0:T(8,128)}, u32[]{:S(2)}, u32[]{:S(2)}) async-start(f32[4,2048,256]{2,1,0:T(8,128)} %bitcast.121), calls=%async_computation.1 | async-start | bytes 16777216 | tf_op jit(solution)/shard_map/all_to_all | solution.py:99
  876.7 8.7 copy-start.5
where the time goes:
time: 910 us; the launch traced here: 906 us
  local copies, waits for them, and re-layouts  374 us (41%)
  other arithmetic  243 us (27%)
  waiting for transfers between devices  227 us (25%)
  matrix products  41.4 us (5%)
  starting transfers between devices  19.7 us (2%)
    all_to_all x1, waiting for transfers between devices, per_device(): lax.all_to_all(part_mix, 'ctx', split_axis=0, concat_axis=1, tiled=True)  162 us
    dot_general x16, other arithmetic, mode_prefix(): jnp.einsum('xbc,bc->xc', decay, contrib_one, precision=lax.Precision.HIGH...  134 us
    gather x2, local copies, waits for them, and re-layouts, medium_mix(): filters[:, jnp.clip(lag, 0, taps - 1)]  125 us
    dynamic_update_slice x32, local copies, waits for them, and re-layouts, modal_local(): lax.map(mode_prefix, (rate_modes, contrib.transpose(1, 0, 2)))  76.3 us
    unnamed x25, local copies, waits for them, and re-layouts  68.7 us
    add x1, other arithmetic, featurize(): total = total + weights[j] * extended[width - 1 - j:width - 1 - j + count]  66.6 us
    all_to_all x1, waiting for transfers between devices, per_device(): lax.all_to_all(lr_input, 'ctx', split_axis=1, concat_axis=0, tiled=True)  64.5 us
    gather x2, local copies, waits for them, and re-layouts, modal_local(): kernel[jnp.maximum(lag, 0)]  25.3 us
  transfers between devices with their start and end apart: 4, of which 2 were waited for; matrix products, arithmetic and copies ran while one was open for 26% of the time, Pallas kernels for 0%

commit v1 on v0

--- a/solution.py
+++ b/solution.py
@@ -5,6 +5,36 @@
 
 TAPS = 128
 SHORT = 7
+
+
+def assign_thing_on_mesh(arr_in, axis_no, x_part):
+    outcome_arr = arr_in.shape
+    y = arr_in.reshape(
+        *outcome_arr[:axis_no], x_part, outcome_arr[axis_no] // x_part, *outcome_arr[axis_no + 1 :]
+    )
+    return jnp.moveaxis(y, axis_no, 0)
+
+
+def shape_bench_over_axis(field, join_dim):
+    work_now = list(field.shape[1:])
+    work_now[join_dim] *= field.shape[0]
+    return jnp.moveaxis(field, 0, join_dim).reshape(work_now)
+
+
+def number_pools(view, along_axis, original, message=0):
+    local_out = lax.axis_index(along_axis)
+    everything = lax.axis_size(along_axis)
+    seen_now, top = (everything, local_out)
+    tall = assign_thing_on_mesh(view, original, seen_now)
+    earlier = tall
+    for ii in range(1, seen_now):
+        finding, r_now = ((top + ii) % seen_now, (top - ii) % seen_now)
+        reached = lax.dynamic_index_in_dim(tall, finding, 0)
+        e_now = map(lambda i0: (i0, (i0 + ii) % seen_now), range(seen_now))
+        v_now = list(e_now)
+        w2 = lax.ppermute(reached, along_axis, v_now)
+        earlier = lax.dynamic_update_slice_in_dim(earlier, w2, r_now, axis=0)
+    return shape_bench_over_axis(earlier, message)
 
 
 def passed_along(shard, axis, by):
@@ -89,7 +119,7 @@
     extended = jnp.concatenate([prior, product], 0)
     mixed = medium_mix(extended, mr_filter)
     lr_input = (lr_gates[:, 1] * query * mixed).astype(jnp.bfloat16)
-    spread = lax.all_to_all(lr_input, "ctx", split_axis=1, concat_axis=0, tiled=True)
+    spread = number_pools(lr_input, "ctx", 1)
     width = spread.shape[1]
     offset = lax.axis_index("ctx") * width
     rate_modes = lax.dynamic_slice_in_dim(lr_rate, offset, width, 0).T

time: 910 us -> 916 us (level)
  waiting for transfers between devices: 227 us -> 201 us
  starting transfers between devices: 19.7 us -> 37.5 us
  local copies, waits for them, and re-layouts: 374 us -> 384 us
    all_to_all x1 -> x0, waiting for transfers between devices: 64.5 us -> none  [per_device(): lax.all_to_all(lr_input, 'ctx', split_axis=1, concat_axis=0, tiled=True)]
    ppermute x0 -> x3, waiting for transfers between devices: none -> 37.7 us  [number_pools(): w2 = lax.ppermute(reached, along_axis, v_now)]
    all_to_all x1, starting transfers between devices: 5.94 us -> 24.2 us  [per_device(): lax.all_to_all(part_mix, 'ctx', split_axis=0, concat_axis=1, tiled=True)]
    dynamic_update_slice x0 -> x4, local copies, waits for them, and re-layouts: none -> 10.6 us  [number_pools(): earlier = lax.dynamic_update_slice_in_dim(earlier, w2, r_now, axis=0)]
    unnamed x25 -> x27, local copies, waits for them, and re-layouts: 68.7 us -> 72.9 us
  transfers between devices with their start and end apart: 4 -> 6, of which waited for: 2 -> 2; matrix products, arithmetic and copies ran while one was open for 26% -> 26% of each run, Pallas kernels for 0% -> 0%
where the time goes in v1:
time: 916 us; the launch traced here: 906 us
  local copies, waits for them, and re-layouts  384 us (42%)
  other arithmetic  241 us (26%)
  waiting for transfers between devices  201 us (22%)
  matrix products  41.6 us (5%)
  starting transfers between devices  37.5 us (4%)
    all_to_all x1, waiting for transfers between devices, per_device(): lax.all_to_all(part_mix, 'ctx', split_axis=0, concat_axis=1, tiled=True)  164 us
    dot_general x16, other arithmetic, mode_prefix(): jnp.einsum('xbc,bc->xc', decay, contrib_one, precision=lax.Precision.HIGH...  134 us
    gather x2, local copies, waits for them, and re-layouts, medium_mix(): filters[:, jnp.clip(lag, 0, taps - 1)]  124 us
    dynamic_update_slice x32, local copies, waits for them, and re-layouts, modal_local(): lax.map(mode_prefix, (rate_modes, contrib.transpose(1, 0, 2)))  76.2 us
    unnamed x27, local copies, waits for them, and re-layouts  72.9 us
    add x1, other arithmetic, featurize(): total = total + weights[j] * extended[width - 1 - j:width - 1 - j + count]  66.5 us
    ppermute x3, waiting for transfers between devices, number_pools(): w2 = lax.ppermute(reached, along_axis, v_now)  37.7 us
    gather x2, local copies, waits for them, and re-layouts, modal_local(): kernel[jnp.maximum(lag, 0)]  25.2 us
  transfers between devices with their start and end apart: 6, of which 2 were waited for; matrix products, arithmetic and copies ran while one was open for 26% of the time, Pallas kernels for 0%

profile of v1, /device:TPU:0, one launch (start us, length us, event | category | flops | bytes accessed | tf_op | source)
XLA Modules:
  0.0 906.3 jit_solution(11276994769572805772)
XLA Ops:
  0.8 5.0 collective-permute-start
  7.3 17.8 %fusion.47 = (bf16[2048,1,1024]{2,1,0:T(2,128)(2,1)}, bf16[2048,1,1024]{2,1,0:T(2,128)(2,1)}) fusion(bf16[2048,2,1024]{2,1,0:T(2,128)(2,1)} %param.12), kind=kLoop, calls=%fused_computation.95 | loop fusion | bytes 16777216 | tf_op jit(solution)/shard_map/slice | solution.py:130
  25.2 17.1 %copy.54 = bf16[2048,3,1024]{0,2,1:T(8,128)(2,1)} copy(bf16[2048,3,1024]{2,0,1:T(8,128)(2,1)} %param.9) | data formatting | bytes 25165824 | tf_op args[0]
  42.4 19.8 %copy.94 = bf16[2048,1,1024]{0,2,1:T(8,128)(2,1)} copy(bf16[2048,1,1024]{2,1,0:T(2,128)(2,1)} %get-tuple-element.70) | data formatting | bytes 8388608
  62.7 66.5 %multiply_add_fusion = f32[2048,3,1024]{0,2,1:T(8,128)} fusion(bf16[2048,3,1024]{0,2,1:T(8,128)(2,1)} %copy.54, bf16[6,3,1024]{0,2,1:T(8,128)(2,1)S(1)} %copy.55, f32[3,1024]{1,0:T(4,128)S(1)} %get-tuple-element.81, f32[3,1024]{1,0:T(4,128)S(1)} %get-tuple-element.82, f32[3,1024]{1,0:T(4,128)S(1)} %get-tuple-element.83, f32[3,1024]{1,0:T(4,128)S(1)} %get-tuple-element.84, ...), kind=kLoop, calls=%fused_computation.15 | loop fusion | flops 239075328 | bytes 37871616 | tf_op jit(solution)/shard_map/add | solution.py:51
  129.3 14.7 %fusion.10 = (bf16[2048,1,1024]{0,2,1:T(8,128)(2,1)S(1)}, f32[2048,1,1024]{0,2,1:T(8,128)}) fusion(f32[2048,3,1024]{0,2,1:T(8,128)} %multiply_add_fusion, bf16[2048,1,1024]{0,2,1:T(8,128)(2,1)} %copy.94), kind=kLoop, calls=%fused_computation.28 | loop fusion | flops 8388608 | bytes 41943040 | tf_op jit(solution)/shard_map/convert_element_type | solution.py:117
  150.1 114.2 %gather_fusion = bf16[32768,64]{1,0:T(8,128)(2,1)} fusion(bf16[64,128]{0,1:T(8,128)(2,1)S(1)} %copy.57, s32[32768]{0:T(1024)S(1)} %broadcast_clamp_fusion), kind=kCustom, calls=%fused_computation | custom fusion | bytes 8519680 | tf_op jit(solution)/shard_map/gather | solution.py:70
  264.3 10.1 %copy.58 = bf16[128,256,64]{1,0,2:T(8,128)(2,1)} copy(bf16[128,256,64]{2,1,0:T(8,128)(2,1)} %bitcast.129) | data formatting | bytes 8388608 | tf_op jit(solution)/shard_map/gather | solution.py:70
  274.5 5.6 copy.99
  280.2 7.9 concatenate.13
  294.2 7.8 fusion.11
  302.0 9.3 %reshape.166 = f32[2048,4,256]{0,2,1:T(8,128)} reshape(f32[16,128,64,16]{1,0,3,2:T(8,128)} %bitcast.125) | data formatting | bytes 16777216 | tf_op jit(solution)/shard_map/reshape | solution.py:73
  311.2 7.2 multiply_convert_fusion
  329.7 16.1 %gather_fusion.1 = f32[4096,256]{1,0:T(8,128)} fusion(f32[64,256]{1,0:T(8,128)S(1)} %bitcast.121, s32[4096]{0:T(1024)S(1)} %broadcast_clamp_fusion.1), kind=kCustom, calls=%fused_computation.1 | custom fusion | bytes 8404992 | tf_op jit(solution)/shard_map/gather | solution.py:85
  345.7 9.1 %copy.61 = f32[64,64,256]{1,0,2:T(8,128)} copy(f32[64,64,256]{2,1,0:T(8,128)} %bitcast.131) | data formatting | bytes 8388608 | tf_op jit(solution)/shard_map/gather | solution.py:85
  355.9 37.7 %collective-permute-done.3 = bf16[1,2048,256]{1,2,0:T(8,128)(2,1)S(1)} collective-permute-done((bf16[1,2048,256]{1,2,0:T(8,128)(2,1)}, bf16[1,2048,256]{1,2,0:T(8,128)(2,1)S(1)}, u32[]{:S(2)}, u32[]{:S(2)}) %collective-permute-start.3) | collective-permute-done | bytes 1048608 | tf_op jit(solution)/shard_map/ppermute | solution.py:35
  397.0 6.2 copy.59
  403.2 7.3 copy.62
  410.5 5.2 fusion.32
  415.8 215.3 %while.11 = (s32[]{:T(128)}, f32[16,128,256]{1,0,2:T(8,128)}, f32[16,128,256]{1,0,2:T(8,128)S(1)}, f32[16,256]{1,0:T(8,128)S(1)}, s32[]{:T(128)}, /*index=5*/s32[]{:T(128)}) while((s32[]{:T(128)}, f32[16,128,256]{1,0,2:T(8,128)}, f32[16,128,256]{1,0,2:T(8,128)S(1)}, f32[16,256]{1,0:T(8,128)S(1)}, s32[]{:T(128)}, ...), condition=%wide.region_1.2_spmd.clone, body=%wide.region_0.1_spmd.clone.sunk | while | flops 16892160 | bytes 1477713 | solution.py:101
  416.1 8.4 multiply_reduce_fusion.3
  429.5 8.4 multiply_reduce_fusion.3
  438.0 4.7 dynamic_update_slice.21
  443.0 8.4 multiply_reduce_fusion.3
  451.5 4.7 dynamic_update_slice.21
  456.4 8.4 multiply_reduce_fusion.3
  464.9 4.7 dynamic_update_slice.21
  469.9 8.4 multiply_reduce_fusion.3
  483.3 8.4 multiply_reduce_fusion.3
  496.8 8.4 multiply_reduce_fusion.3
  510.2 8.4 multiply_reduce_fusion.3
  523.7 8.4 multiply_reduce_fusion.3
  537.2 8.4 multiply_reduce_fusion.3
  550.6 8.4 multiply_reduce_fusion.3
  564.1 8.4 multiply_reduce_fusion.3
  577.5 8.4 multiply_reduce_fusion.3
  591.0 8.4 multiply_reduce_fusion.3
  604.4 8.4 multiply_reduce_fusion.3
  617.9 8.4 multiply_reduce_fusion.3
  631.1 18.0 %fusion.28 = f32[256,64,128]{2,1,0:T(8,128)} fusion(f32[16,128,256]{1,0,2:T(8,128)} %get-tuple-element.37, f32[16,256]{0,1:T(8,128)S(1)} %copy.63, f32[64]{0:T(128)S(1)} %broadcast_add_fusion, f32[16,256]{0,1:T(8,128)S(1)} %copy.60), kind=kOutput, calls=%fused_computation.52 | convolution fusion | flops 403177472 | bytes 10518784 | tf_op jit(solution)/shard_map/brc,trc->btc/dot_general | solution.py:108
  649.1 10.5 %bitcast_add_fusion.1 = f32[128,64,256]{0,1,2:T(8,128)} fusion(f32[256,64,128]{2,1,0:T(8,128)} %fusion.28, bf16[128,64,256]{0,1,2:T(8,128)(2,1)S(1)} %copy-done.1, f32[64,64,256]{1,0,2:T(8,128)} %copy.61, pred[64,64]{1,0:T(8,128)(4,1)S(1)} %subtract_compare_fusion), kind=kOutput, calls=%fused_computation.37 | convolution fusion | flops 1613758464 | bytes 25169920 | tf_op jit(solution)/shard_map/tsc,bsc->btc/dot_general | solution.py:87
  659.6 9.2 %copy.67 = f32[128,64,256]{2,1,0:T(8,128)} copy(f32[128,64,256]{0,1,2:T(8,128)} %bitcast_add_fusion.1) | data formatting | bytes 16777216 | tf_op jit(solution)/shard_map/add | solution.py:109
  668.9 24.2 %all-to-all-start = ((f32[4,2048,256]{2,1,0:T(8,128)}), f32[4,2048,256]{2,1,0:T(8,128)}, u32[]{:S(2)}, u32[]{:S(2)}) async-start(f32[4,2048,256]{2,1,0:T(8,128)} %bitcast.127), calls=%async_computation | async-start | bytes 16777216 | tf_op jit(solution)/shard_map/all_to_all | solution.py:129
  693.1 19.9 %copy.95 = bf16[2048,1,1024]{0,2,1:T(8,128)(2,1)} copy(bf16[2048,1,1024]{2,1,0:T(2,128)(2,1)} %get-tuple-element.69) | data formatting | bytes 8388608
  713.0 163.7 %all-to-all-done = f32[4,2048,256]{2,1,0:T(8,128)} async-done(((f32[4,2048,256]{2,1,0:T(8,128)}), f32[4,2048,256]{2,1,0:T(8,128)}, u32[]{:S(2)}, u32[]{:S(2)}) %all-to-all-start) | async-done | bytes 8388640 | tf_op jit(solution)/shard_map/all_to_all | solution.py:129
  876.6 8.7 copy.68
  885.4 14.3 %fusion.14 = bf16[2048,1024]{0,1:T(8,128)(2,1)} fusion(f32[2048,4,256]{0,2,1:T(8,128)} %copy.68, f32[128,8,16,128]{3,2,1,0:T(8,128)} %bitcast.126, f32[2048,1,1024]{0,2,1:T(8,128)} %get-tuple-element.68, bf16[2048,1,1024]{0,2,1:T(8,128)(2,1)} %copy.95, f32[1024]{0:T(1024)S(1)} %copy-done.6), kind=kLoop, calls=%fused_computation.35 | loop fusion | flops 16777216 | bytes 33558528 | tf_op jit(solution)/shard_map/convert_element_type | solution.py:130
  899.7 6.4 copy.69
  (167 shorter events, 96.8 us)
Async XLA Ops:
  0.8 61.5 %collective-permute-start = (bf16[6,3,1024]{2,0,1:T(8,128)(2,1)S(1)}, bf16[6,3,1024]{2,0,1:T(8,128)(2,1)S(1)}, u32[]{:S(2)}, u32[]{:S(2)}) collective-permute-start(bf16[6,3,1024]{2,0,1:T(8,128)(2,1)S(1)} %slice.70), channel_id=1, source_target_pairs={{0,4},{4,8},{8,12},{1,5},{5,9},{9,13},{2,6},{6,10},{10,14},{3,7},{... | collective-permute-start | bytes 110600 | tf_op jit(solution)/shard_map/ppermute | solution.py:43
  129.3 20.7 %copy-start.5 = (bf16[64,128]{1,0:T(8,128)(2,1)S(1)}, bf16[64,128]{1,0:T(8,128)(2,1)}, u32[]{:S(2)}) copy-start(bf16[64,128]{1,0:T(8,128)(2,1)} %param.11) | copy-start | bytes 49156
  143.9 2.0 copy-start
  146.1 134.0 %collective-permute-start.1 = (bf16[127,1024]{0,1:T(8,128)(2,1)S(1)}, bf16[127,1024]{0,1:T(8,128)(2,1)S(1)}, u32[]{:S(2)}, u32[]{:S(2)}) collective-permute-start(bf16[127,1024]{0,1:T(8,128)(2,1)S(1)} %slice_bitcast_fusion.1), channel_id=1, source_target_pairs={{0,4},{4,8},{8,12},{1,5},{5,9},{9,13},{2,6},{6,10},{10,14},{3,7},{... | collective-permute-start | bytes 780296 | tf_op jit(solution)/shard_map/ppermute | solution.py:43
  288.1 6.1 copy-start.3
  288.1 6.1 copy-start.4
  318.4 2.0 copy-start.2
  322.2 32.6 %collective-permute-start.2 = (bf16[1,2048,256]{1,2,0:T(8,128)(2,1)}, bf16[1,2048,256]{1,2,0:T(8,128)(2,1)S(1)}, u32[]{:S(2)}, u32[]{:S(2)}) collective-permute-start(bf16[1,2048,256]{1,2,0:T(8,128)(2,1)} %get-tuple-element.73), channel_id=1, source_target_pairs={{0,4},{4,8},{8,12},{12,0},{1,5},{5,9},{9,13},{13,1},{2,6},{6,10},{... | collective-permute-start | bytes 3145736 | tf_op jit(solution)/shard_map/ppermute | solution.py:35
  324.9 68.7 %collective-permute-start.3 = (bf16[1,2048,256]{1,2,0:T(8,128)(2,1)}, bf16[1,2048,256]{1,2,0:T(8,128)(2,1)S(1)}, u32[]{:S(2)}, u32[]{:S(2)}) collective-permute-start(bf16[1,2048,256]{1,2,0:T(8,128)(2,1)} %get-tuple-element.72), channel_id=1, source_target_pairs={{0,8},{4,12},{8,0},{12,4},{1,9},{5,13},{9,1},{13,5},{2,10},{6,14},... | collective-permute-start | bytes 3145736 | tf_op jit(solution)/shard_map/ppermute | solution.py:35
  326.8 67.9 %collective-permute-start.4 = (bf16[1,2048,256]{1,2,0:T(8,128)(2,1)}, bf16[1,2048,256]{1,2,0:T(8,128)(2,1)}, u32[]{:S(2)}, u32[]{:S(2)}) collective-permute-start(bf16[1,2048,256]{1,2,0:T(8,128)(2,1)} %get-tuple-element.71), channel_id=1, source_target_pairs={{0,12},{4,0},{8,4},{12,8},{1,13},{5,1},{9,5},{13,9},{2,14},{6,2},{... | collective-permute-start | bytes 3145736 | tf_op jit(solution)/shard_map/ppermute | solution.py:35
  631.0 18.1 %copy-start.1 = (bf16[128,64,256]{0,1,2:T(8,128)(2,1)S(1)}, bf16[128,64,256]{0,1,2:T(8,128)(2,1)}, u32[]{:S(2)}) copy-start(bf16[128,64,256]{0,1,2:T(8,128)(2,1)} %copy.62) | copy-start | bytes 12582916
  668.9 207.8 %all-to-all-start = ((f32[4,2048,256]{2,1,0:T(8,128)}), f32[4,2048,256]{2,1,0:T(8,128)}, u32[]{:S(2)}, u32[]{:S(2)}) async-start(f32[4,2048,256]{2,1,0:T(8,128)} %bitcast.127), calls=%async_computation | async-start | bytes 16777216 | tf_op jit(solution)/shard_map/all_to_all | solution.py:129
  876.6 8.7 copy-start.6
